TPU v7x, 256 devices: a whole 4x4x8 slice. The times are simulated.
256 devices in a mesh: dp: 4 (over y), section: 16 (over z, x_lo), tensor: 4 (over x_hi, core).
Axes of the slice: x: 4 (x_hi: 2, x_lo: 2; x = x_hi * 2 + x_lo), y: 4, z: 8, core: 2. Of those that a mesh axis runs over, the one named last changes fastest.
Arguments:
- saved_input: bfloat16 [16, 2, 512, 8192], P('section', None, ('dp', 'tensor')), may hold values from -6 to 6
- kv_grad: bfloat16 [16, 2, 512, 2048], P('section', None, 'dp', 'tensor'), may hold values from -1.5 to 1.5
- kv_weight: bfloat16 [16, 8192, 2048], P('section', 'dp', 'tensor'), may hold values from -0.0625 to 0.0625
- norm_gain: bfloat16 [16, 8192], P('section'), may hold values from 0.5 to 1.5
- top_grad: bfloat16 [2, 512, 8192], P(None, ('dp', 'tensor')), may hold values from -1.5 to 1.5
- noise_salt: int32 [1], replicated, may hold values from 0 to 1073741823
- step_counter: int32 [1], replicated, may hold values from 0 to 999999
Outputs:
- input_grads: bfloat16 [16, 2, 512, 8192], P('section', None, ('dp', 'tensor'))
- weight_grads: float32 [16, 8192, 2048], P('section', 'dp', 'tensor')
All inputs are finite; a program needn't handle non-finite values.
Results may differ from a plain program's by a relative error of at most 0.012.
Values may be sent and summed in bfloat16 or wider, within the bound.
No kernel may reach another device: no remote copies, remote signals or barrier semaphores. Data moves between devices by JAX's collectives and lax.ppermute only.
A program may use at most 128 MiB of HBM per device.

v0:
```python
import jax
import jax.numpy as jnp
from jax import lax
from jax.sharding import PartitionSpec as P


def mix_bits(salt, counter, layer, group, index):
    h = (
        index * jnp.int32(-1640531535)
        + salt * jnp.int32(374761393)
        + counter * jnp.int32(668265263)
    )
    h = h + layer * jnp.int32(-1028477379) + group * jnp.int32(1274126177)
    h = h ^ lax.shift_right_logical(h, jnp.int32(16))
    h = h * jnp.int32(2146121005)
    h = h ^ lax.shift_right_logical(h, jnp.int32(15))
    h = h * jnp.int32(-2073254261)
    h = h ^ lax.shift_right_logical(h, jnp.int32(16))
    return lax.shift_right_logical(h, jnp.int32(8)).astype(jnp.float32) * (1.0 / 16777216.0)


def dither(term, salt, counter, layer, group, index):
    noise = mix_bits(salt, counter, layer, group, index)
    moved = term * (1.0 + (noise - 0.5) * 0.5)
    return lax.optimization_barrier(moved.astype(jnp.bfloat16)).astype(jnp.float32)


def later_sum(branch_path):
    n_sec = lax.axis_size("section")
    m, t, d = branch_path.shape
    chunks = lax.all_to_all(
        branch_path.astype(jnp.bfloat16)[None], "section", 3, 0, tiled=True
    ).astype(jnp.float32)
    acc = jnp.zeros(chunks.shape[1:], jnp.float32)
    outs = [None] * n_sec
    for s in range(n_sec - 1, -1, -1):
        outs[s] = acc
        acc = acc + chunks[s]
    stacked = jnp.stack(outs).astype(jnp.bfloat16)
    back = lax.all_to_all(stacked, "section", 0, 3, tiled=True)
    return back[0].astype(jnp.float32)


def shards(saved_input, kv_grad, kv_weight, norm_gain, top_grad, noise_salt, step_counter):
    salt = noise_salt[0]
    counter = step_counter[0]
    layer = lax.axis_index("section")
    n_dp = lax.axis_size("dp")
    n_t = lax.axis_size("tensor")
    my_p = lax.axis_index("dp")
    my_t = lax.axis_index("tensor")
    cotan = kv_grad[0]
    weight = kv_weight[0]
    rows_p, width_t = weight.shape
    total_cols = width_t * n_t
    mb, tok_dev, d_model = saved_input.shape[1:]
    input_float = saved_input[0].astype(jnp.float32)
    inverse_scale = lax.rsqrt(jnp.mean(input_float * input_float, axis=-1, keepdims=True) + 1e-05)
    centered_input = input_float * inverse_scale
    gain_float = norm_gain[0].astype(jnp.float32)
    normed_values = (centered_input * gain_float).astype(jnp.bfloat16)
    cotan_all = lax.all_gather(cotan, "dp", axis=1, tiled=True)
    part = jnp.einsum("mtk,dk->mtd", cotan_all, weight, preferred_element_type=jnp.float32).astype(
        jnp.bfloat16
    )
    part = part.reshape(mb, n_dp * n_t, tok_dev, rows_p).transpose(1, 0, 2, 3)
    got = lax.all_to_all(part, ("dp", "tensor"), 0, 0, tiled=True)
    got = got.reshape(n_dp, n_t, mb, tok_dev, rows_p).astype(jnp.float32)
    normed_grad = got[:, 0]
    for t in range(1, n_t):
        normed_grad = normed_grad + got[:, t]
    normed_grad = normed_grad.transpose(1, 2, 0, 3).reshape(mb, tok_dev, d_model)
    hidden_gradient = normed_grad * gain_float
    branch_path = inverse_scale * (
        hidden_gradient
        - centered_input * jnp.mean(hidden_gradient * centered_input, axis=-1, keepdims=True)
    )
    later = later_sum(branch_path)
    grad_in = (top_grad.astype(jnp.float32) + branch_path + later).astype(jnp.bfloat16)
    nrm = normed_values.reshape(mb, tok_dev, n_dp, rows_p).transpose(2, 0, 1, 3)
    nrm = lax.all_to_all(nrm, "dp", 0, 0, tiled=True)
    nrm = lax.all_gather(nrm, "tensor", axis=0, tiled=False)
    cot = cotan_all.reshape(mb, n_dp, n_t, tok_dev, width_t)
    terms = jnp.einsum("tpmid,mptik->pdk", nrm, cot, preferred_element_type=jnp.float32)
    row_ids = my_p * jnp.int32(rows_p) + jnp.arange(rows_p, dtype=jnp.int32)
    index = (
        row_ids[:, None] * jnp.int32(total_cols)
        + my_t * jnp.int32(width_t)
        + jnp.arange(width_t, dtype=jnp.int32)[None, :]
    )
    wsum = jnp.zeros((rows_p, width_t), jnp.float32)
    for g in range(n_dp):
        wsum = wsum + dither(terms[g], salt, counter, layer, jnp.int32(g), index)
    return (grad_in[None], wsum[None])


def solution(mesh):
    placed = (
        P("section", None, ("dp", "tensor"), None),
        P("section", None, "dp", "tensor"),
        P("section", "dp", "tensor"),
        P("section", None),
        P(None, ("dp", "tensor"), None),
        P(),
        P(),
    )
    return jax.shard_map(
        shards,
        mesh=mesh,
        in_specs=placed,
        out_specs=(P("section", None, ("dp", "tensor"), None), P("section", "dp", "tensor")),
        check_vma=False,
    )
```

profile of v0, /device:TPU:8, one launch (start us, length us, event | category | flops | bytes accessed | tf_op | source)
XLA Modules:
  0.0 288.4 jit_solution(17948738188843804011)
XLA Ops:
  7.9 30.3 %all-gather.5.cloned.1.call-done = bf16[1,2,512,512]{3,2,1,0:T(8,128)(2,1)} async-done(((bf16[1,2,128,512]{3,2,1,0:T(8,128)(2,1)}), bf16[1,2,512,512]{3,2,1,0:T(8,128)(2,1)}) %all-gather.5.cloned.1.call-update) | async-done | bytes 1048592 | tf_op jit(solution)/shard_map/all_gather | solution.py:62
  38.2 3.6 %convolution_convert_fusion = bf16[2,512,2048]{2,1,0:T(8,128)(2,1)S(1)} fusion(bf16[1,2048,512]{2,1,0:T(8,128)(2,1)S(1)} %copy-done, bf16[1,2,512,512]{3,2,1,0:T(8,128)(2,1)} %all-gather.5.cloned.1.call-done), kind=kOutput, calls=%fused_computation.60 | convolution fusion | flops 2149580800 | bytes 7340032 | tf_op jit(solution)/shard_map/mtk,dk->mtd/dot_general | solution.py:63
  41.8 2.3 copy.237
  44.1 7.6 %all-to-all-start = ((bf16[16,2,32,2048]{3,2,1,0:T(8,128)(2,1)}), bf16[16,2,32,2048]{3,2,1,0:T(8,128)(2,1)}, u32[]{:S(2)}, u32[]{:S(2)}) async-start(bf16[16,2,32,2048]{3,2,1,0:T(8,128)(2,1)} %bitcast.145), calls=%async_computation | async-start | bytes 8388608 | tf_op jit(solution)/shard_map/all_to_all | solution.py:67
  51.9 2.7 reshape.107
  55.0 47.1 %all-to-all-done = bf16[16,2,32,2048]{3,2,1,0:T(8,128)(2,1)} async-done(((bf16[16,2,32,2048]{3,2,1,0:T(8,128)(2,1)}), bf16[16,2,32,2048]{3,2,1,0:T(8,128)(2,1)}, u32[]{:S(2)}, u32[]{:S(2)}) %all-to-all-start) | async-done | bytes 4194336 | tf_op jit(solution)/shard_map/all_to_all | solution.py:67
  102.0 3.4 %bitcast_convert_fusion = f32[4,4,2,32,2048]{4,3,2,1,0:T(8,128)S(1)} fusion(bf16[16,2,32,2048]{3,2,1,0:T(8,128)(2,1)} %all-to-all-done), kind=kLoop, calls=%fused_computation.121 | loop fusion | flops 2097152 | bytes 12582912 | tf_op jit(solution)/shard_map/convert_element_type | solution.py:68
  105.5 3.0 %multiply_reduce_fusion = (f32[2,32]{1,0:T(2,128)S(1)}, f32[4,1,2,32,2048]{4,3,2,1,0:T(8,128)S(1)}, bf16[4,2,32,2048]{3,2,1,0:T(8,128)(2,1)}) fusion(f32[2,32,4,2048]{3,2,1,0:T(4,128)S(1)} %copy-done.4, f32[2,32]{1,0:T(2,128)S(1)} %add_rsqrt_fusion, f32[4,2048]{1,0:T(4,128)S(1)} %reshape.106, f32[4,4,2,32,2048]{4,3,2,1,0:T(8,128)S(1)} %bitcast_convert_fusion), kind=kLoop, calls=%fused_computation.78 | loop fusion | flops 4718528 | bytes 13664768 | tf_op jit(solution)/shard_map/reduce_sum | solution.py:76
  108.4 5.9 %all-to-all-start.3 = ((bf16[4,2,32,2048]{3,2,1,0:T(8,128)(2,1)}), bf16[4,2,32,2048]{3,2,1,0:T(8,128)(2,1)}, u32[]{:S(2)}, u32[]{:S(2)}) async-start(bf16[4,2,32,2048]{3,2,1,0:T(8,128)(2,1)} %get-tuple-element.20), calls=%async_computation.3 | async-start | bytes 2097152 | tf_op jit(solution)/shard_map/all_to_all | solution.py:81
  114.3 2.7 copy.102
  117.0 3.6 %reshape.101 = f32[1,2,32,8192]{3,2,1,0:T(8,128)} reshape(f32[2,32,4,2048]{3,2,1,0:T(4,128)} %copy.102) | data formatting | bytes 4194304 | tf_op jit(solution)/shard_map/reshape | solution.py:72
  120.6 3.1 %multiply_convert_fusion.1 = bf16[1,2,32,8192]{3,2,1,0:T(8,128)(2,1)} fusion(f32[1,2,32,8192]{3,2,1,0:T(8,128)} %reshape.101, bf16[1,2,32,8192]{3,2,1,0:T(8,128)(2,1)S(1)} %copy-done.2, f32[2,32]{1,0:T(2,128)S(1)} %broadcast_multiply_fusion, f32[8192]{0:T(1024)S(1)} %bitcast.151, f32[2,32]{1,0:T(2,128)S(1)} %add_rsqrt_fusion), kind=kLoop, calls=%fused_computation.77 | loop fusion | flops 3670016 | bytes 4227584 | tf_op jit(solution)/shard_map/convert_element_type | solution.py:32
  123.7 9.2 %copy.105 = bf16[1,2,32,8192]{2,1,0,3:T(2,128)(2,1)} copy(bf16[1,2,32,8192]{3,2,1,0:T(8,128)(2,1)} %multiply_convert_fusion.1) | data formatting | bytes 2097152 | tf_op jit(solution)/shard_map/convert_element_type | solution.py:32
  132.8 9.9 %reshape.147 = bf16[16,2,16384]{2,1,0:T(2,128)(2,1)} reshape(bf16[8192,1,2,32]{3,2,1,0:T(2,128)(2,1)} %bitcast.143) | data formatting | bytes 2097152
  142.8 7.2 %all-to-all-start.1 = ((bf16[16,2,16384]{2,1,0:T(2,128)(2,1)}), bf16[16,2,16384]{2,1,0:T(2,128)(2,1)}, u32[]{:S(2)}, u32[]{:S(2)}) async-start(bf16[16,2,16384]{2,1,0:T(2,128)(2,1)} %reshape.147), calls=%async_computation.1 | async-start | bytes 2097152 | tf_op jit(solution)/shard_map/all_to_all | solution.py:31
  150.7 27.2 %all-to-all-done.1 = bf16[16,2,16384]{2,1,0:T(2,128)(2,1)} async-done(((bf16[16,2,16384]{2,1,0:T(2,128)(2,1)}), bf16[16,2,16384]{2,1,0:T(2,128)(2,1)}, u32[]{:S(2)}, u32[]{:S(2)}) %all-to-all-start.1) | async-done | bytes 1048608 | tf_op jit(solution)/shard_map/all_to_all | solution.py:31
  177.9 10.0 %reshape.148 = bf16[8192,1,2,32]{3,2,1,0:T(2,128)(2,1)} reshape(bf16[16,2,16384]{2,1,0:T(2,128)(2,1)} %all-to-all-done.1) | data formatting | bytes 2097152
  187.9 9.0 %copy.106 = bf16[1,2,32,8192]{3,2,1,0:T(8,128)(2,1)} copy(bf16[1,2,32,8192]{2,1,0,3:T(2,128)(2,1)} %bitcast.144) | data formatting | bytes 2097152 | tf_op jit(solution)/shard_map/all_to_all | solution.py:31
  196.9 1.6 copy.154
  198.6 1.8 fusion.61
  211.0 7.5 %stack.3 = bf16[16,2,32,512]{3,0,2,1:T(8,128)(2,1)} concatenate(bf16[1,2,32,512]{3,0,2,1:T(2,128)(2,1)S(1)} %fusion.53, bf16[1,2,32,512]{3,0,2,1:T(2,128)(2,1)S(1)} %copy.122, bf16[1,2,32,512]{3,0,2,1:T(2,128)(2,1)} %copy.123, bf16[1,2,32,512]{3,0,2,1:T(2,128)(2,1)S(1)} %copy.124, bf16[1,2,32,512]{3,0,2,1:T(2,128)(2,1)} %copy.125, bf16[1,2,32,512]{3,0,2,1:T(2,128)(2,1)} %copy.126, ...), dimensions={0} | concatenate | bytes 2097152 | tf_op jit(solution)/shard_map/stack | solution.py:39
  218.5 2.8 copy.135
  221.3 4.6 %all-to-all-start.2 = ((bf16[16,2,32,512]{3,2,1,0:T(8,128)(2,1)}), bf16[16,2,32,512]{3,2,1,0:T(8,128)(2,1)}, u32[]{:S(2)}, u32[]{:S(2)}) async-start(bf16[16,2,32,512]{3,2,1,0:T(8,128)(2,1)} %copy.135), calls=%async_computation.2 | async-start | bytes 2097152 | tf_op jit(solution)/shard_map/all_to_all | solution.py:40
  227.2 1.6 copy.153
  228.7 23.9 %all-to-all-done.2 = bf16[16,2,32,512]{3,2,1,0:T(8,128)(2,1)} async-done(((bf16[16,2,32,512]{3,2,1,0:T(8,128)(2,1)}), bf16[16,2,32,512]{3,2,1,0:T(8,128)(2,1)}, u32[]{:S(2)}, u32[]{:S(2)}) %all-to-all-start.2) | async-done | bytes 1048608 | tf_op jit(solution)/shard_map/all_to_all | solution.py:40
  252.6 1.5 convert_bitcast_fusion
  254.1 2.5 copy.136
  256.7 2.9 %reshape.110 = f32[2,32,8192]{2,1,0:T(8,128)} reshape(f32[1,2,32,16,512]{4,3,2,1,0:T(8,128)} %copy.136) | data formatting | bytes 4194304 | tf_op jit(solution)/shard_map/convert_element_type | solution.py:41
  259.6 3.5 %fusion.49 = bf16[1,2,32,8192]{3,2,1,0:T(8,128)(2,1)} fusion(f32[2,32,8192]{2,1,0:T(8,128)} %reshape.110, bf16[1,2,32,8192]{3,2,1,0:T(8,128)(2,1)S(1)} %copy-done.2, f32[2,32,8192]{2,1,0:T(8,128)S(1)} %bitcast.146, bf16[2,32,8192]{2,1,0:T(8,128)(2,1)} %param.11, f32[2,32]{1,0:T(2,128)S(1)} %broadcast_multiply_fusion, f32[8192]{0:T(1024)S(1)} %bitcast.152, ...), kind=kLoop, calls=%fused_computation.80 | loop fusion | flops 5242880 | bytes 7373312 | tf_op jit(solution)/shard_map/broadcast_in_dim | solution.py:94
  263.1 4.9 %convolution_bitcast_fusion = f32[4,2048,512]{2,1,0:T(8,128)S(1)} fusion(bf16[4,4,2,32,2048]{4,3,2,1,0:T(8,128)(2,1)} %bitcast.154, bf16[2,4,4,32,512]{4,3,2,1,0:T(8,128)(2,1)} %bitcast.155), kind=kOutput, calls=%fused_computation | convolution fusion | flops 2147483648 | bytes 22020096 | tf_op jit(solution)/shard_map/tpmid,mptik->pdk/dot_general | solution.py:84
  268.0 10.4 %fusion.39 = (bf16[2048,512]{1,0:T(8,128)(2,1)S(1)}, bf16[2048,512]{1,0:T(8,128)(2,1)S(1)}, bf16[2048,512]{1,0:T(8,128)(2,1)S(1)}, bf16[2048,512]{1,0:T(8,128)(2,1)S(1)}) fusion(f32[4,2048,512]{2,1,0:T(8,128)S(1)} %convolution_bitcast_fusion, s32[]{:T(128)S(6)} %mul.216, s32[]{:T(128)} %bitcast.37, s32[]{:T(128)} %bitcast.36, s32[2048]{0:T(1024)S(1)} %multiply_add_fusion), kind=kLoop, calls=%fused_computation.59 | loop fusion | flops 75497472 | bytes 25174028 | tf_op jit(solution)/shard_map/convert_element_type | solution.py:25
  278.4 3.2 %add_bitcast_fusion = f32[1,2048,512]{2,1,0:T(8,128)} fusion(bf16[2048,512]{1,0:T(8,128)(2,1)S(1)} %get-tuple-element.17, bf16[2048,512]{1,0:T(8,128)(2,1)S(1)} %get-tuple-element.18, bf16[2048,512]{1,0:T(8,128)(2,1)S(1)} %get-tuple-element.19, bf16[2048,512]{1,0:T(8,128)(2,1)S(1)} %get-tuple-element.16), kind=kLoop, calls=%fused_computation.54 | loop fusion | flops 7340032 | bytes 12582912 | tf_op jit(solution)/shard_map/broadcast_in_dim | solution.py:94
  (53 shorter events, 12.5 us)
Async XLA Ops:
  7.2 31.0 %copy-start = (bf16[1,2048,512]{2,1,0:T(8,128)(2,1)S(1)}, bf16[1,2048,512]{2,1,0:T(8,128)(2,1)}, u32[]{:S(2)}) copy-start(bf16[1,2048,512]{2,1,0:T(8,128)(2,1)} %param.9) | copy-start | bytes 6291460
  7.2 31.0 %all-gather.5.cloned.1.call-start = ((), (), s32[]{:S(2)}) async-start(), calls=%async_computation.4 | async-start | bytes 1310720 | tf_op jit(solution)/shard_map/all_gather | solution.py:62
  44.1 7.6 %copy-start.7 = (bf16[1,8192]{1,0:T(2,128)(2,1)S(1)}, bf16[1,8192]{1,0:T(2,128)(2,1)}, u32[]{:S(2)}) copy-start(bf16[1,8192]{1,0:T(2,128)(2,1)} %param.10) | copy-start | bytes 49156
  44.1 7.8 %copy-start.2 = (bf16[1,2,32,8192]{3,2,1,0:T(8,128)(2,1)S(1)}, bf16[1,2,32,8192]{3,2,1,0:T(8,128)(2,1)}, u32[]{:S(2)}) copy-start(bf16[1,2,32,8192]{3,2,1,0:T(8,128)(2,1)} %param.7) | copy-start | bytes 3145732
  44.1 57.9 %all-to-all-start = ((bf16[16,2,32,2048]{3,2,1,0:T(8,128)(2,1)}), bf16[16,2,32,2048]{3,2,1,0:T(8,128)(2,1)}, u32[]{:S(2)}, u32[]{:S(2)}) async-start(bf16[16,2,32,2048]{3,2,1,0:T(8,128)(2,1)} %bitcast.145), calls=%async_computation | async-start | bytes 8388608 | tf_op jit(solution)/shard_map/all_to_all | solution.py:67
  51.8 68.8 %copy-start.5 = (f32[1,8192]{1,0:T(1,128)}, f32[1,8192]{1,0:T(1,128)S(1)}, u32[]{:S(2)}) copy-start(f32[1,8192]{1,0:T(1,128)S(1)} %convert_element_type.151) | copy-start | bytes 98308
  102.0 3.4 %copy-start.4 = (f32[2,32,4,2048]{3,2,1,0:T(4,128)S(1)}, f32[2,32,4,2048]{3,2,1,0:T(4,128)}, u32[]{:S(2)}) copy-start(f32[2,32,4,2048]{3,2,1,0:T(4,128)} %reshape.107) | copy-start | bytes 6291460
  108.4 34.3 %all-to-all-start.3 = ((bf16[4,2,32,2048]{3,2,1,0:T(8,128)(2,1)}), bf16[4,2,32,2048]{3,2,1,0:T(8,128)(2,1)}, u32[]{:S(2)}, u32[]{:S(2)}) async-start(bf16[4,2,32,2048]{3,2,1,0:T(8,128)(2,1)} %get-tuple-element.20), calls=%async_computation.3 | async-start | bytes 2097152 | tf_op jit(solution)/shard_map/all_to_all | solution.py:81
  142.8 35.1 %all-to-all-start.1 = ((bf16[16,2,16384]{2,1,0:T(2,128)(2,1)}), bf16[16,2,16384]{2,1,0:T(2,128)(2,1)}, u32[]{:S(2)}, u32[]{:S(2)}) async-start(bf16[16,2,16384]{2,1,0:T(2,128)(2,1)} %reshape.147), calls=%async_computation.1 | async-start | bytes 2097152 | tf_op jit(solution)/shard_map/all_to_all | solution.py:31
  150.0 113.2 %all-gather.7.cloned.1.call-start = ((), (), s32[]{:S(2)}) async-start(), calls=%async_computation.5 | async-start | bytes 5242880 | tf_op jit(solution)/shard_map/all_gather | solution.py:82
  221.3 31.3 %all-to-all-start.2 = ((bf16[16,2,32,512]{3,2,1,0:T(8,128)(2,1)}), bf16[16,2,32,512]{3,2,1,0:T(8,128)(2,1)}, u32[]{:S(2)}, u32[]{:S(2)}) async-start(bf16[16,2,32,512]{3,2,1,0:T(8,128)(2,1)} %copy.135), calls=%async_computation.2 | async-start | bytes 2097152 | tf_op jit(solution)/shard_map/all_to_all | solution.py:40
  254.1 5.5 %copy-start.6 = (f32[1,8192]{1,0:T(1,128)S(1)}, f32[1,8192]{1,0:T(1,128)}, u32[]{:S(2)}) copy-start(f32[1,8192]{1,0:T(1,128)} %copy-done.5) | copy-start | bytes 98308
  256.7 2.9 %copy-start.3 = (f32[4,2,4,8,2048]{4,3,0,2,1:T(8,128)S(1)}, f32[4,2,4,8,2048]{4,3,0,2,1:T(8,128)}, u32[]{:S(2)}) copy-start(f32[4,2,4,8,2048]{4,3,0,2,1:T(8,128)} %copy.153) | copy-start | bytes 6291460
  278.4 3.2 %copy-start.1 = (bf16[1,2048,512]{2,1,0:T(8,128)(2,1)S(1)}, bf16[1,2048,512]{2,1,0:T(8,128)(2,1)}, u32[]{:S(2)}) copy-start(bf16[1,2048,512]{2,1,0:T(8,128)(2,1)} %param.9) | copy-start | bytes 6291460
Sparse Core Ops, SparseCore 0:
  9.8 28.3 all-gather.4
  152.6 46.6 all-gather.6
where the time goes:
time: 290 us; the launch traced here: 288 us
  waiting for transfers between devices  130 us (45%)
  local copies, waits for them, and re-layouts  80.4 us (28%)
  other arithmetic  28.9 us (10%)
  starting transfers between devices  25.5 us (9%)
  between operations  15.6 us (5%)
  matrix products  8.46 us (3%)
    all_to_all x1, waiting for transfers between devices, shards(): got = lax.all_to_all(part, ('dp', 'tensor'), 0, 0, tiled=True)  47.1 us
    all_gather x1, waiting for transfers between devices, shards(): cotan_all = lax.all_gather(cotan, 'dp', axis=1, tiled=True)  30.3 us
    all_to_all x1, waiting for transfers between devices, later_sum(): lax.all_to_all(branch_path.astype(jnp.bfloat16)[None], 'section', 3, 0, t...  27.2 us
    all_to_all x1, waiting for transfers between devices, later_sum(): back = lax.all_to_all(stacked, 'section', 0, 3, tiled=True)  23.9 us
    unnamed x20, local copies, waits for them, and re-layouts  21.6 us
    another operation x3, local copies, waits for them, and re-layouts, later_sum(): stacked = jnp.stack(outs).astype(jnp.bfloat16)  11 us
    convert_element_type x1, other arithmetic, dither(): moved.astype(jnp.bfloat16)  10.4 us
    another operation x14, local copies, waits for them, and re-layouts  9.33 us
  transfers between devices with their start and end apart: 6, of which 4 were waited for; matrix products, arithmetic and copies ran while one was open for 30% of the time, Pallas kernels for 0%

commit v1 on v0

--- a/solution.py
+++ b/solution.py
@@ -59,7 +59,12 @@
     centered_input = input_float * inverse_scale
     gain_float = norm_gain[0].astype(jnp.float32)
     normed_values = (centered_input * gain_float).astype(jnp.bfloat16)
-    cotan_all = lax.all_gather(cotan, "dp", axis=1, tiled=True)
+    cotan_all = jnp.concatenate(
+        jax.lax.all_to_all(
+            jnp.stack([cotan for _ in range(jax.lax.axis_size("dp"))], 0), "dp", 0, 0
+        ),
+        1,
+    )
     part = jnp.einsum("mtk,dk->mtd", cotan_all, weight, preferred_element_type=jnp.float32).astype(
         jnp.bfloat16
     )

time: 290 us -> 279 us (0.962)
  waiting for transfers between devices: 130 us -> 98.8 us
  blocking collectives: 0 us -> 18.3 us
    all_gather x1 -> x0, waiting for transfers between devices: 30.3 us -> none  [shards(): cotan_all = lax.all_gather(cotan, 'dp', axis=1, tiled=True)]
    all_to_all x0 -> x1, blocking collectives: none -> 18.3 us  [shards(): jax.lax.all_to_all(jnp.stack([cotan for _ in range(jax.lax.axis_size('dp'...]
    another operation x14 -> x15, local copies, waits for them, and re-layouts: 9.33 us -> 10.5 us
    unnamed x20 -> x22, local copies, waits for them, and re-layouts: 21.6 us -> 22.6 us
  transfers between devices with their start and end apart: 6 -> 5, of which waited for: 4 -> 3; matrix products, arithmetic and copies ran while one was open for 30% -> 31% of each run, Pallas kernels for 0% -> 0%
where the time goes in v1:
time: 279 us; the launch traced here: 277 us
  waiting for transfers between devices  98.8 us (35%)
  local copies, waits for them, and re-layouts  82.5 us (30%)
  other arithmetic  28.9 us (10%)
  starting transfers between devices  26 us (9%)
  blocking collectives  18.3 us (7%)
  between operations  15.6 us (6%)
  matrix products  7.26 us (3%)
    all_to_all x1, waiting for transfers between devices, shards(): got = lax.all_to_all(part, ('dp', 'tensor'), 0, 0, tiled=True)  47.1 us
    all_to_all x1, waiting for transfers between devices, later_sum(): lax.all_to_all(branch_path.astype(jnp.bfloat16)[None], 'section', 3, 0, t...  27.2 us
    all_to_all x1, waiting for transfers between devices, later_sum(): back = lax.all_to_all(stacked, 'section', 0, 3, tiled=True)  23.8 us
    unnamed x22, local copies, waits for them, and re-layouts  22.6 us
    all_to_all x1, blocking collectives, shards(): jax.lax.all_to_all(jnp.stack([cotan for _ in range(jax.lax.axis_size('dp'...  18.3 us
    another operation x3, local copies, waits for them, and re-layouts, later_sum(): stacked = jnp.stack(outs).astype(jnp.bfloat16)  11 us
    convert_element_type x1, other arithmetic, dither(): moved.astype(jnp.bfloat16)  10.4 us
    another operation x14, local copies, waits for them, and re-layouts  9.27 us
  transfers between devices with their start and end apart: 5, of which 3 were waited for; matrix products, arithmetic and copies ran while one was open for 31% of the time, Pallas kernels for 0%

profile of v1, /device:TPU:8, one launch (start us, length us, event | category | flops | bytes accessed | tf_op | source)
XLA Modules:
  0.0 277.3 jit_solution(15659947959631619552)
XLA Ops:
  8.4 18.3 %all_to_all.33 = bf16[4,2,128,512]{3,2,1,0:T(8,128)(2,1)S(1)} all-to-all(bf16[4,2,128,512]{3,2,1,0:T(8,128)(2,1)S(1)} %stack.5), channel_id=1, replica_groups=mesh['dp'=4,'section'=16,'tensor'=4] {'dp'}, dimensions={0} | all-to-all | bytes 2097152 | tf_op jit(solution)/shard_map/all_to_all | solution.py:63
  27.8 2.4 convolution_convert_fusion
  30.2 2.3 copy.272
  32.5 6.5 %all-to-all-start.1 = ((bf16[16,2,32,2048]{3,2,1,0:T(8,128)(2,1)}), bf16[16,2,32,2048]{3,2,1,0:T(8,128)(2,1)}, u32[]{:S(2)}, u32[]{:S(2)}) async-start(bf16[16,2,32,2048]{3,2,1,0:T(8,128)(2,1)} %bitcast.148), calls=%async_computation.1 | async-start | bytes 8388608 | tf_op jit(solution)/shard_map/all_to_all | solution.py:72
  39.2 2.7 reshape.112
  42.2 47.1 %all-to-all-done.1 = bf16[16,2,32,2048]{3,2,1,0:T(8,128)(2,1)} async-done(((bf16[16,2,32,2048]{3,2,1,0:T(8,128)(2,1)}), bf16[16,2,32,2048]{3,2,1,0:T(8,128)(2,1)}, u32[]{:S(2)}, u32[]{:S(2)}) %all-to-all-start.1) | async-done | bytes 4194336 | tf_op jit(solution)/shard_map/all_to_all | solution.py:72
  89.3 3.4 %bitcast_convert_fusion = f32[4,4,2,32,2048]{4,3,2,1,0:T(8,128)S(1)} fusion(bf16[16,2,32,2048]{3,2,1,0:T(8,128)(2,1)} %all-to-all-done.1), kind=kLoop, calls=%fused_computation.120 | loop fusion | flops 2097152 | bytes 12582912 | tf_op jit(solution)/shard_map/convert_element_type | solution.py:73
  92.7 3.0 %multiply_reduce_fusion = (f32[2,32]{1,0:T(2,128)S(1)}, f32[4,1,2,32,2048]{4,3,2,1,0:T(8,128)S(1)}, bf16[4,2,32,2048]{3,2,1,0:T(8,128)(2,1)}) fusion(f32[2,32,4,2048]{3,2,1,0:T(4,128)S(1)} %copy-done.4, f32[2,32]{1,0:T(2,128)S(1)} %add_rsqrt_fusion, f32[4,2048]{1,0:T(4,128)S(1)} %reshape.111, f32[4,4,2,32,2048]{4,3,2,1,0:T(8,128)S(1)} %bitcast_convert_fusion), kind=kLoop, calls=%fused_computation.78 | loop fusion | flops 4718528 | bytes 13664768 | tf_op jit(solution)/shard_map/reduce_sum | solution.py:81
  95.7 5.9 %all-to-all-start.4 = ((bf16[4,2,32,2048]{3,2,1,0:T(8,128)(2,1)}), bf16[4,2,32,2048]{3,2,1,0:T(8,128)(2,1)}, u32[]{:S(2)}, u32[]{:S(2)}) async-start(bf16[4,2,32,2048]{3,2,1,0:T(8,128)(2,1)} %get-tuple-element.20), calls=%async_computation.4 | async-start | bytes 2097152 | tf_op jit(solution)/shard_map/all_to_all | solution.py:86
  101.6 2.7 copy.136
  104.2 3.7 %reshape.107 = f32[1,2,32,8192]{3,2,1,0:T(8,128)} reshape(f32[2,32,4,2048]{3,2,1,0:T(4,128)} %copy.136) | data formatting | bytes 4194304 | tf_op jit(solution)/shard_map/reshape | solution.py:77
  107.9 3.1 %multiply_convert_fusion.1 = bf16[1,2,32,8192]{3,2,1,0:T(8,128)(2,1)} fusion(f32[1,2,32,8192]{3,2,1,0:T(8,128)} %reshape.107, bf16[1,2,32,8192]{3,2,1,0:T(8,128)(2,1)S(1)} %copy-done.2, f32[2,32]{1,0:T(2,128)S(1)} %broadcast_multiply_fusion, f32[8192]{0:T(1024)S(1)} %bitcast.156, f32[2,32]{1,0:T(2,128)S(1)} %add_rsqrt_fusion), kind=kLoop, calls=%fused_computation.77 | loop fusion | flops 3670016 | bytes 4227584 | tf_op jit(solution)/shard_map/convert_element_type | solution.py:32
  111.0 9.2 %copy.139 = bf16[1,2,32,8192]{2,1,0,3:T(2,128)(2,1)} copy(bf16[1,2,32,8192]{3,2,1,0:T(8,128)(2,1)} %multiply_convert_fusion.1) | data formatting | bytes 2097152 | tf_op jit(solution)/shard_map/convert_element_type | solution.py:32
  120.1 9.9 %reshape.150 = bf16[16,2,16384]{2,1,0:T(2,128)(2,1)} reshape(bf16[8192,1,2,32]{3,2,1,0:T(2,128)(2,1)} %bitcast.146) | data formatting | bytes 2097152
  130.0 9.0 %all-to-all-start.2 = ((bf16[16,2,16384]{2,1,0:T(2,128)(2,1)}), bf16[16,2,16384]{2,1,0:T(2,128)(2,1)}, u32[]{:S(2)}, u32[]{:S(2)}) async-start(bf16[16,2,16384]{2,1,0:T(2,128)(2,1)} %reshape.150), calls=%async_computation.2 | async-start | bytes 2097152 | tf_op jit(solution)/shard_map/all_to_all | solution.py:31
  139.8 27.2 %all-to-all-done.2 = bf16[16,2,16384]{2,1,0:T(2,128)(2,1)} async-done(((bf16[16,2,16384]{2,1,0:T(2,128)(2,1)}), bf16[16,2,16384]{2,1,0:T(2,128)(2,1)}, u32[]{:S(2)}, u32[]{:S(2)}) %all-to-all-start.2) | async-done | bytes 1048608 | tf_op jit(solution)/shard_map/all_to_all | solution.py:31
  167.0 10.0 %reshape.151 = bf16[8192,1,2,32]{3,2,1,0:T(2,128)(2,1)} reshape(bf16[16,2,16384]{2,1,0:T(2,128)(2,1)} %all-to-all-done.2) | data formatting | bytes 2097152
  177.0 9.0 %copy.140 = bf16[1,2,32,8192]{3,2,1,0:T(8,128)(2,1)} copy(bf16[1,2,32,8192]{2,1,0,3:T(2,128)(2,1)} %bitcast.147) | data formatting | bytes 2097152 | tf_op jit(solution)/shard_map/all_to_all | solution.py:31
  186.0 1.6 copy.189
  187.7 1.8 fusion.60
  199.9 7.5 %stack.6 = bf16[16,2,32,512]{3,0,2,1:T(8,128)(2,1)} concatenate(bf16[1,2,32,512]{3,0,2,1:T(2,128)(2,1)S(1)} %fusion.52, bf16[1,2,32,512]{3,0,2,1:T(2,128)(2,1)S(1)} %copy.156, bf16[1,2,32,512]{3,0,2,1:T(2,128)(2,1)} %copy.157, bf16[1,2,32,512]{3,0,2,1:T(2,128)(2,1)S(1)} %copy.158, bf16[1,2,32,512]{3,0,2,1:T(2,128)(2,1)} %copy.159, bf16[1,2,32,512]{3,0,2,1:T(2,128)(2,1)} %copy.160, ...), dimensions={0} | concatenate | bytes 2097152 | tf_op jit(solution)/shard_map/stack | solution.py:39
  207.4 2.8 copy.169
  210.2 4.6 %all-to-all-start.3 = ((bf16[16,2,32,512]{3,2,1,0:T(8,128)(2,1)}), bf16[16,2,32,512]{3,2,1,0:T(8,128)(2,1)}, u32[]{:S(2)}, u32[]{:S(2)}) async-start(bf16[16,2,32,512]{3,2,1,0:T(8,128)(2,1)} %copy.169), calls=%async_computation.3 | async-start | bytes 2097152 | tf_op jit(solution)/shard_map/all_to_all | solution.py:40
  216.1 1.6 copy.188
  217.7 23.8 %all-to-all-done.3 = bf16[16,2,32,512]{3,2,1,0:T(8,128)(2,1)} async-done(((bf16[16,2,32,512]{3,2,1,0:T(8,128)(2,1)}), bf16[16,2,32,512]{3,2,1,0:T(8,128)(2,1)}, u32[]{:S(2)}, u32[]{:S(2)}) %all-to-all-start.3) | async-done | bytes 1048608 | tf_op jit(solution)/shard_map/all_to_all | solution.py:40
  241.5 1.5 convert_bitcast_fusion
  243.0 2.5 copy.170
  245.6 2.9 %reshape.115 = f32[2,32,8192]{2,1,0:T(8,128)} reshape(f32[1,2,32,16,512]{4,3,2,1,0:T(8,128)} %copy.170) | data formatting | bytes 4194304 | tf_op jit(solution)/shard_map/convert_element_type | solution.py:41
  248.5 3.5 %fusion.49 = bf16[1,2,32,8192]{3,2,1,0:T(8,128)(2,1)} fusion(f32[2,32,8192]{2,1,0:T(8,128)} %reshape.115, bf16[1,2,32,8192]{3,2,1,0:T(8,128)(2,1)S(1)} %copy-done.2, f32[2,32,8192]{2,1,0:T(8,128)S(1)} %bitcast.149, bf16[2,32,8192]{2,1,0:T(8,128)(2,1)} %param.11, f32[2,32]{1,0:T(2,128)S(1)} %broadcast_multiply_fusion, f32[8192]{0:T(1024)S(1)} %bitcast.157, ...), kind=kLoop, calls=%fused_computation.80 | loop fusion | flops 5242880 | bytes 7373312 | tf_op jit(solution)/shard_map/broadcast_in_dim | solution.py:99
  252.0 4.9 %convolution_bitcast_fusion = f32[4,2048,512]{2,1,0:T(8,128)S(1)} fusion(bf16[4,4,2,32,2048]{4,3,2,1,0:T(8,128)(2,1)} %bitcast.160, bf16[2,4,4,32,512]{4,3,2,0,1:T(8,128)(2,1)} %bitcast.154), kind=kOutput, calls=%fused_computation | convolution fusion | flops 2147483648 | bytes 22020096 | tf_op jit(solution)/shard_map/tpmid,mptik->pdk/dot_general | solution.py:89
  256.9 10.4 %fusion.39 = (bf16[2048,512]{1,0:T(8,128)(2,1)S(1)}, bf16[2048,512]{1,0:T(8,128)(2,1)S(1)}, bf16[2048,512]{1,0:T(8,128)(2,1)S(1)}, bf16[2048,512]{1,0:T(8,128)(2,1)S(1)}) fusion(f32[4,2048,512]{2,1,0:T(8,128)S(1)} %convolution_bitcast_fusion, s32[]{:T(128)S(6)} %mul.216, s32[]{:T(128)} %bitcast.40, s32[]{:T(128)} %bitcast.39, s32[2048]{0:T(1024)S(1)} %multiply_add_fusion), kind=kLoop, calls=%fused_computation.59 | loop fusion | flops 75497472 | bytes 25174028 | tf_op jit(solution)/shard_map/convert_element_type | solution.py:25
  267.3 3.2 %add_bitcast_fusion = f32[1,2048,512]{2,1,0:T(8,128)} fusion(bf16[2048,512]{1,0:T(8,128)(2,1)S(1)} %get-tuple-element.17, bf16[2048,512]{1,0:T(8,128)(2,1)S(1)} %get-tuple-element.18, bf16[2048,512]{1,0:T(8,128)(2,1)S(1)} %get-tuple-element.19, bf16[2048,512]{1,0:T(8,128)(2,1)S(1)} %get-tuple-element.16), kind=kLoop, calls=%fused_computation.54 | loop fusion | flops 7340032 | bytes 12582912 | tf_op jit(solution)/shard_map/broadcast_in_dim | solution.py:99
  (55 shorter events, 13.9 us)
Async XLA Ops:
  7.2 20.6 %copy-start = (bf16[1,2048,512]{2,1,0:T(8,128)(2,1)S(1)}, bf16[1,2048,512]{2,1,0:T(8,128)(2,1)}, u32[]{:S(2)}) copy-start(bf16[1,2048,512]{2,1,0:T(8,128)(2,1)} %param.9) | copy-start | bytes 6291460
  26.7 1.1 copy-start.5
  32.5 6.5 %copy-start.8 = (bf16[1,8192]{1,0:T(2,128)(2,1)S(1)}, bf16[1,8192]{1,0:T(2,128)(2,1)}, u32[]{:S(2)}) copy-start(bf16[1,8192]{1,0:T(2,128)(2,1)} %param.10) | copy-start | bytes 49156
  32.5 6.7 %copy-start.2 = (bf16[1,2,32,8192]{3,2,1,0:T(8,128)(2,1)S(1)}, bf16[1,2,32,8192]{3,2,1,0:T(8,128)(2,1)}, u32[]{:S(2)}) copy-start(bf16[1,2,32,8192]{3,2,1,0:T(8,128)(2,1)} %param.7) | copy-start | bytes 3145732
  32.5 56.8 %all-to-all-start.1 = ((bf16[16,2,32,2048]{3,2,1,0:T(8,128)(2,1)}), bf16[16,2,32,2048]{3,2,1,0:T(8,128)(2,1)}, u32[]{:S(2)}, u32[]{:S(2)}) async-start(bf16[16,2,32,2048]{3,2,1,0:T(8,128)(2,1)} %bitcast.148), calls=%async_computation.1 | async-start | bytes 8388608 | tf_op jit(solution)/shard_map/all_to_all | solution.py:72
  39.1 68.8 %copy-start.6 = (f32[1,8192]{1,0:T(1,128)}, f32[1,8192]{1,0:T(1,128)S(1)}, u32[]{:S(2)}) copy-start(f32[1,8192]{1,0:T(1,128)S(1)} %convert_element_type.151) | copy-start | bytes 98308
  89.3 3.4 %copy-start.4 = (f32[2,32,4,2048]{3,2,1,0:T(4,128)S(1)}, f32[2,32,4,2048]{3,2,1,0:T(4,128)}, u32[]{:S(2)}) copy-start(f32[2,32,4,2048]{3,2,1,0:T(4,128)} %reshape.112) | copy-start | bytes 6291460
  95.7 34.4 %all-to-all-start.4 = ((bf16[4,2,32,2048]{3,2,1,0:T(8,128)(2,1)}), bf16[4,2,32,2048]{3,2,1,0:T(8,128)(2,1)}, u32[]{:S(2)}, u32[]{:S(2)}) async-start(bf16[4,2,32,2048]{3,2,1,0:T(8,128)(2,1)} %get-tuple-element.20), calls=%async_computation.4 | async-start | bytes 2097152 | tf_op jit(solution)/shard_map/all_to_all | solution.py:86
  130.0 37.0 %all-to-all-start.2 = ((bf16[16,2,16384]{2,1,0:T(2,128)(2,1)}), bf16[16,2,16384]{2,1,0:T(2,128)(2,1)}, u32[]{:S(2)}, u32[]{:S(2)}) async-start(bf16[16,2,16384]{2,1,0:T(2,128)(2,1)} %reshape.150), calls=%async_computation.2 | async-start | bytes 2097152 | tf_op jit(solution)/shard_map/all_to_all | solution.py:31
  139.0 113.0 %all-gather.3.cloned.1.call-start = ((), (), s32[]{:S(2)}) async-start(), calls=%async_computation.5 | async-start | bytes 5242880 | tf_op jit(solution)/shard_map/all_gather | solution.py:87
  210.2 31.3 %all-to-all-start.3 = ((bf16[16,2,32,512]{3,2,1,0:T(8,128)(2,1)}), bf16[16,2,32,512]{3,2,1,0:T(8,128)(2,1)}, u32[]{:S(2)}, u32[]{:S(2)}) async-start(bf16[16,2,32,512]{3,2,1,0:T(8,128)(2,1)} %copy.169), calls=%async_computation.3 | async-start | bytes 2097152 | tf_op jit(solution)/shard_map/all_to_all | solution.py:40
  243.0 5.5 %copy-start.7 = (f32[1,8192]{1,0:T(1,128)S(1)}, f32[1,8192]{1,0:T(1,128)}, u32[]{:S(2)}) copy-start(f32[1,8192]{1,0:T(1,128)} %copy-done.6) | copy-start | bytes 98308
  245.6 2.9 %copy-start.3 = (f32[4,2,4,8,2048]{4,3,0,2,1:T(8,128)S(1)}, f32[4,2,4,8,2048]{4,3,0,2,1:T(8,128)}, u32[]{:S(2)}) copy-start(f32[4,2,4,8,2048]{4,3,0,2,1:T(8,128)} %copy.188) | copy-start | bytes 6291460
  267.3 3.2 %copy-start.1 = (bf16[1,2048,512]{2,1,0:T(8,128)(2,1)S(1)}, bf16[1,2048,512]{2,1,0:T(8,128)(2,1)}, u32[]{:S(2)}) copy-start(bf16[1,2048,512]{2,1,0:T(8,128)(2,1)} %param.9) | copy-start | bytes 6291460
Sparse Core Ops, SparseCore 0:
  141.7 46.6 all-gather.2
